TPU v7x, 512 devices: a whole 4x4x16 slice. The times are simulated.
512 devices in a mesh: ctx: 64 (over x_hi, z, core), mp: 8 (over x_lo, y).
Axes of the slice: x: 4 (x_hi: 2, x_lo: 2; x = x_hi * 2 + x_lo), y: 4, z: 16, core: 2. Of those that a mesh axis runs over, the one named last changes fastest.
Arguments:
- queries: bfloat16 [4096, 8192], P('ctx', 'mp'), may hold values from -8 to 8
- keys: bfloat16 [4096, 1024], P('ctx', 'mp'), may hold values from -8 to 8
- values: bfloat16 [4096, 1024], P('ctx', 'mp'), may hold values from -6 to 6
- positions: int32 [4096], P('ctx'), may hold values from 0 to 4095, as said below
- x_normed: bfloat16 [4096, 8192], P('ctx', 'mp'), may hold values from -6 to 6
- w_gate: bfloat16 [8192, 16384], P('mp', 'ctx'), may hold values from -0.0625 to 0.0625
- w_up: bfloat16 [8192, 16384], P('mp', 'ctx'), may hold values from -0.0625 to 0.0625
Outputs:
- attended: bfloat16 [4096, 8192], P('ctx', 'mp')
- mlp_hidden: bfloat16 [4096, 16384], P('mp', 'ctx')
Inputs may be any that keep to these rules, and one draw needn't show every extreme that they name: `positions`: each position of 0 to 4095 appears exactly once.
All inputs are finite; a program needn't handle non-finite values.
Results may differ from a plain program's by a relative error of at most 0.02.
Values may be sent and summed in bfloat16 or wider, within the bound.
No kernel may reach another device: no remote copies, remote signals or barrier semaphores. Data moves between devices by JAX's collectives and lax.ppermute only.
A program may use at most 64 MiB of HBM per device.

v0:
```python
import jax
import jax.numpy as jnp
from jax import lax
from jax.sharding import PartitionSpec as P

HEAD = 128


def per_device(queries, keys, values, positions, x_normed, w_gate, w_up):
    tok_rows = queries.shape[0]
    local_heads = queries.shape[1] // HEAD
    local_kv = keys.shape[1] // HEAD
    group = local_heads // local_kv
    scale = HEAD ** (-0.5)
    query_four = queries.reshape(tok_rows, local_kv, group, HEAD)
    top_run = jnp.full((local_kv, group, tok_rows), -1e30, jnp.float32)
    k_piece = lax.all_gather(keys, "ctx", axis=0, tiled=True)
    v_piece = lax.all_gather(values, "ctx", axis=0, tiled=True)
    k_pos = lax.all_gather(positions, "ctx", axis=0, tiled=True)
    count = k_piece.shape[0]
    k_three = k_piece.reshape(count, local_kv, HEAD)
    v_three = v_piece.reshape(count, local_kv, HEAD)
    scores = (
        jnp.einsum("tgjd,sgd->gjts", query_four, k_three, preferred_element_type=jnp.float32)
        * scale
    )
    visible = k_pos[None, :] <= positions[:, None]
    piece_top = jnp.max(jnp.where(visible, scores, jnp.float32(-1e30)), axis=-1)
    top_new = jnp.maximum(top_run, piece_top)
    weights = jnp.where(visible, jnp.exp(scores - top_new[..., None]), jnp.float32(0.0))
    total_new = jnp.sum(weights, axis=-1)
    mixed = jnp.einsum(
        "gjts,sgd->gjtd", weights.astype(jnp.bfloat16), v_three, preferred_element_type=jnp.float32
    )
    final_state = (top_new, total_new, mixed)
    top_run, total_run, accum = final_state
    normed = accum / total_run[..., None]
    attended = (
        jnp.transpose(normed, (2, 0, 1, 3))
        .reshape(tok_rows, local_heads * HEAD)
        .astype(jnp.bfloat16)
    )
    hidden_cols = w_gate.shape[1]
    both_weights = jnp.concatenate((w_gate, w_up), axis=1)
    block_terms = jnp.dot(
        lax.all_gather(x_normed, "ctx", axis=0, tiled=True),
        both_weights,
        preferred_element_type=jnp.float32,
    ).astype(jnp.bfloat16)
    summed = lax.psum_scatter(
        block_terms.astype(jnp.float32).astype(jnp.bfloat16), "mp", scatter_dimension=0, tiled=True
    ).astype(jnp.float32)
    gate = summed[:, :hidden_cols]
    up = summed[:, hidden_cols:]
    mlp_hidden = (jax.nn.silu(gate) * up).astype(jnp.bfloat16)
    return (attended, mlp_hidden)


def solution(mesh):
    return jax.shard_map(
        per_device,
        mesh=mesh,
        in_specs=(
            P("ctx", "mp"),
            P("ctx", "mp"),
            P("ctx", "mp"),
            P("ctx"),
            P("ctx", "mp"),
            P("mp", "ctx"),
            P("mp", "ctx"),
        ),
        out_specs=(P("ctx", "mp"), P("mp", "ctx")),
        check_vma=False,
    )
```

profile of v0, /device:TPU:1, one launch (start us, length us, event | category | flops | bytes accessed | tf_op | source)
XLA Modules:
  0.0 528.0 jit_solution(817598872555930921)
XLA Ops:
  7.2 0.0 all-gather.8.cloned.1.call-start
  7.2 0.7 all-gather.8.cloned.1.call-update
  7.9 0.0 all-gather.4.cloned.1.call-start
  8.0 0.7 all-gather.4.cloned.1.call-update
  8.7 0.0 all-gather.6.cloned.1.call-start
  8.7 0.7 all-gather.6.cloned.1.call-update
  9.4 0.0 reduce-scatter.2.cloned.1.call-start
  9.5 172.6 %all-gather.8.cloned.1.call-done = bf16[4096,1024]{1,0:T(8,128)(2,1)} async-done(((bf16[64,1024]{1,0:T(8,128)(2,1)}), bf16[4096,1024]{1,0:T(8,128)(2,1)}) %all-gather.8.cloned.1.call-update) | async-done | bytes 8388624 | tf_op jit(solution)/shard_map/all_gather | solution.py:46
  182.1 10.2 %fusion.5 = bf16[4096,512]{0,1:T(8,128)(2,1)} fusion(bf16[4096,1024]{1,0:T(8,128)(2,1)} %all-gather.8.cloned.1.call-done, bf16[1024,256]{1,0:T(8,128)(2,1)} %param.13, bf16[1024,256]{1,0:T(8,128)(2,1)} %param.12), kind=kOutput, calls=%fused_computation.8 | convolution fusion | flops 4299161600 | bytes 13631488 | tf_op jit(solution)/shard_map/dot_general | solution.py:45
  192.3 1.3 dynamic-slice
  194.3 0.3 dynamic-update-slice
  194.5 251.6 %all-reduce = s32[4096]{0:T(1024)S(1)} all-reduce(s32[4096]{0:T(1024)S(1)} %dynamic-update-slice), channel_id=1, replica_groups=mesh['ctx'=64,'mp'=8] {'ctx'}, use_global_device_ids=true, to_apply=%add | all-reduce | flops 4096 | bytes 32768
  446.1 0.2 broadcast_compare_fusion
  446.4 2.9 fusion
  449.3 3.2 copy-done.1
  452.5 2.4 fusion.3
  454.9 5.6 %all-gather.6.cloned.1.call-done = bf16[4096,128]{1,0:T(8,128)(2,1)} async-done(((bf16[64,128]{1,0:T(8,128)(2,1)}), bf16[4096,128]{1,0:T(8,128)(2,1)}) %all-gather.6.cloned.1.call-update) | async-done | bytes 1048592 | tf_op jit(solution)/shard_map/all_gather | solution.py:18
  460.6 5.2 fusion.16
  465.7 0.1 copy.12
  465.8 0.7 copy.23
  466.5 52.7 %reduce-scatter.2.cloned.1.call-done = bf16[512,512]{0,1:T(8,128)(2,1)} async-done(((bf16[4096,512]{0,1:T(8,128)(2,1)}), bf16[512,512]{0,1:T(8,128)(2,1)}) %reduce-scatter.2.cloned.1.call-update) | async-done | bytes 524304 | tf_op jit(solution)/shard_map/reduce_scatter | solution.py:50
  519.3 1.2 convert_element_type.36
  520.4 0.2 fusion.25
  520.6 0.8 copy.13
  (9 shorter events, 0.1 us)
Async XLA Ops:
  7.2 439.2 %copy-start = (bf16[64,1024]{1,0:T(8,128)(2,1)S(1)}, bf16[64,1024]{1,0:T(8,128)(2,1)}, u32[]{:S(2)}) copy-start(bf16[64,1024]{1,0:T(8,128)(2,1)} %param.7) | copy-start | bytes 393220
  7.2 174.9 %all-gather.8.cloned.1.call-start = ((), (), s32[]{:S(2)}) async-start(), calls=%async_computation.3 | async-start | bytes 8519680 | tf_op jit(solution)/shard_map/all_gather | solution.py:46
  7.9 438.4 %all-gather.4.cloned.1.call-start = ((), (), s32[]{:S(2)}) async-start(), calls=%async_computation.1 | async-start | bytes 1064960 | tf_op jit(solution)/shard_map/all_gather | solution.py:17
  8.7 451.9 %all-gather.6.cloned.1.call-start = ((), (), s32[]{:S(2)}) async-start(), calls=%async_computation.2 | async-start | bytes 1064960 | tf_op jit(solution)/shard_map/all_gather | solution.py:18
  9.4 184.9 %copy-start.2 = (s32[64]{0:T(128)S(1)}, s32[64]{0:T(128)}, u32[]{:S(2)}) copy-start(s32[64]{0:T(128)} %param.10) | copy-start | bytes 772
  9.4 509.9 %reduce-scatter.2.cloned.1.call-start = ((), (), s32[]{:S(2)}) async-start(), calls=%async_computation.4 | async-start | bytes 4718592 | tf_op jit(solution)/shard_map/reduce_scatter | solution.py:50
  449.3 3.2 copy-start.1
Sparse Core Ops, SparseCore 0:
  11.3 170.7 all-gather.7
  185.3 135.2 all-gather.3
  323.9 136.6 all-gather.5
  463.3 55.9 reduce-scatter.1
where the time goes:
time: 528 us
  blocking collectives  252 us (48%)
  waiting for transfers between devices  233 us (44%)
  matrix products  18.3 us (3%)
  between operations  14.5 us (3%)
  local copies, waits for them, and re-layouts  6.38 us (1%)
    unnamed x1, blocking collectives  252 us
    all_gather x1, waiting for transfers between devices, per_device(): lax.all_gather(x_normed, 'ctx', axis=0, tiled=True)  173 us
    reduce_scatter x1, waiting for transfers between devices, per_device(): lax.psum_scatter(block_terms.astype(jnp.float32).astype(jnp.bfloat16), 'm...  52.7 us
  transfers between devices with their start and end apart: 4, of which 3 were waited for; matrix products, arithmetic and copies ran while one was open for 4% of the time, Pallas kernels for 0%

commit v1 on v0

--- a/solution.py
+++ b/solution.py
@@ -4,6 +4,13 @@
 from jax.sharding import PartitionSpec as P
 
 HEAD = 128
+
+
+def trace_the_wires(vec, dim_at):
+    return jnp.concatenate(
+        lax.all_to_all(jnp.stack([vec for _ in range(lax.axis_size("ctx"))], 0), "ctx", 0, 0),
+        dim_at,
+    )
 
 
 def per_device(queries, keys, values, positions, x_normed, w_gate, w_up):
@@ -43,9 +50,7 @@
     hidden_cols = w_gate.shape[1]
     both_weights = jnp.concatenate((w_gate, w_up), axis=1)
     block_terms = jnp.dot(
-        lax.all_gather(x_normed, "ctx", axis=0, tiled=True),
-        both_weights,
-        preferred_element_type=jnp.float32,
+        trace_the_wires(x_normed, 0), both_weights, preferred_element_type=jnp.float32
     ).astype(jnp.bfloat16)
     summed = lax.psum_scatter(
         block_terms.astype(jnp.float32).astype(jnp.bfloat16), "mp", scatter_dimension=0, tiled=True

time: 528 us -> 702 us (1.33)
  waiting for transfers between devices: 233 us -> 373 us
  starting transfers between devices: 0.15 us -> 20 us
    all_to_all x0 -> x1, waiting for transfers between devices: none -> 371 us  [trace_the_wires(): lax.all_to_all(jnp.stack([vec for _ in range(lax.axis_size('ctx'))], 0),...]
    all_gather x1 -> x0, waiting for transfers between devices: 173 us -> none  [per_device(): lax.all_gather(x_normed, 'ctx', axis=0, tiled=True)]
    reduce_scatter x1, waiting for transfers between devices: 52.7 us -> 0.01 us  [per_device(): lax.psum_scatter(block_terms.astype(jnp.float32).astype(jnp.bfloat16), 'm...]
    all_to_all x0 -> x1, starting transfers between devices: none -> 19.9 us  [trace_the_wires(): lax.all_to_all(jnp.stack([vec for _ in range(lax.axis_size('ctx'))], 0),...]
  transfers between devices with their start and end apart: 4 -> 4, of which waited for: 3 -> 1; matrix products, arithmetic and copies ran while one was open for 4% -> 3% of each run, Pallas kernels for 0% -> 0%
where the time goes in v1:
time: 702 us; the launch traced here: 697 us
  waiting for transfers between devices  373 us (53%)
  blocking collectives  255 us (36%)
  starting transfers between devices  20 us (3%)
  matrix products  17.6 us (3%)
  between operations  16.2 us (2%)
  local copies, waits for them, and re-layouts  11.6 us (2%)
    all_to_all x1, waiting for transfers between devices, trace_the_wires(): lax.all_to_all(jnp.stack([vec for _ in range(lax.axis_size('ctx'))], 0),...  371 us
    unnamed x1, blocking collectives  255 us
    all_to_all x1, starting transfers between devices, trace_the_wires(): lax.all_to_all(jnp.stack([vec for _ in range(lax.axis_size('ctx'))], 0),...  19.9 us
  transfers between devices with their start and end apart: 4, of which 1 were waited for; matrix products, arithmetic and copies ran while one was open for 3% of the time, Pallas kernels for 0%

profile of v1, /device:TPU:1, one launch (start us, length us, event | category | flops | bytes accessed | tf_op | source)
XLA Modules:
  0.0 697.3 jit_solution(9690208061225657952)
XLA Ops:
  8.0 5.2 stack.2
  13.2 19.9 %all-to-all-start = ((bf16[64,64,1024]{2,1,0:T(8,128)(2,1)}), bf16[64,64,1024]{2,1,0:T(8,128)(2,1)}, u32[]{:S(2)}, u32[]{:S(2)}) async-start(bf16[64,64,1024]{2,1,0:T(8,128)(2,1)} %stack.2), calls=%async_computation | async-start | bytes 16777216 | tf_op jit(solution)/shard_map/all_to_all | solution.py:11
  33.2 0.0 all-gather.3.cloned.1.call-start
  33.2 0.7 all-gather.3.cloned.1.call-update
  33.9 0.0 all-gather.5.cloned.1.call-start
  34.0 0.7 all-gather.5.cloned.1.call-update
  34.7 0.0 reduce-scatter.2.cloned.1.call-start
  34.7 371.5 %all-to-all-done = bf16[64,64,1024]{2,1,0:T(8,128)(2,1)} async-done(((bf16[64,64,1024]{2,1,0:T(8,128)(2,1)}), bf16[64,64,1024]{2,1,0:T(8,128)(2,1)}, u32[]{:S(2)}, u32[]{:S(2)}) %all-to-all-start) | async-done | bytes 8388640 | tf_op jit(solution)/shard_map/all_to_all | solution.py:11
  406.2 9.6 %fusion.5 = bf16[4096,512]{0,1:T(8,128)(2,1)} fusion(bf16[4096,1024]{1,0:T(8,128)(2,1)} %bitcast.9, bf16[1024,256]{1,0:T(8,128)(2,1)S(1)} %copy-done.3, bf16[1024,256]{1,0:T(8,128)(2,1)S(1)} %copy-done.4), kind=kOutput, calls=%fused_computation.8 | convolution fusion | flops 4299161600 | bytes 13631488 | tf_op jit(solution)/shard_map/dot_general | solution.py:52
  415.8 0.0 reduce-scatter.2.cloned.1.call-update
  415.8 1.3 dynamic-slice
  417.7 0.3 dynamic-update-slice
  418.0 254.9 %all-reduce = s32[4096]{0:T(1024)S(1)} all-reduce(s32[4096]{0:T(1024)S(1)} %dynamic-update-slice), channel_id=1, replica_groups=mesh['ctx'=64,'mp'=8] {'ctx'}, use_global_device_ids=true, to_apply=%add | all-reduce | flops 4096 | bytes 32768
  672.9 0.2 broadcast_compare_fusion
  673.1 0.0 all-gather.3.cloned.1.call-done
  673.1 2.9 fusion
  676.1 3.2 copy-done.1
  679.3 2.4 fusion.3
  681.7 5.1 fusion.16
  686.9 0.1 copy.12
  687.0 0.7 copy.23
  687.6 1.2 convert_element_type.36
  688.8 0.2 fusion.25
  689.0 0.8 copy.13
  (13 shorter events, 0.0 us)
Async XLA Ops:
  8.0 665.1 %copy-start = (bf16[64,1024]{1,0:T(8,128)(2,1)S(1)}, bf16[64,1024]{1,0:T(8,128)(2,1)}, u32[]{:S(2)}) copy-start(bf16[64,1024]{1,0:T(8,128)(2,1)} %param.7) | copy-start | bytes 393220
  13.2 392.9 %copy-start.3 = (bf16[1024,256]{1,0:T(8,128)(2,1)S(1)}, bf16[1024,256]{1,0:T(8,128)(2,1)}, u32[]{:S(2)}) copy-start(bf16[1024,256]{1,0:T(8,128)(2,1)} %param.13) | copy-start | bytes 1572868
  13.2 392.9 %copy-start.4 = (bf16[1024,256]{1,0:T(8,128)(2,1)S(1)}, bf16[1024,256]{1,0:T(8,128)(2,1)}, u32[]{:S(2)}) copy-start(bf16[1024,256]{1,0:T(8,128)(2,1)} %param.12) | copy-start | bytes 1572868
  13.2 392.9 %all-to-all-start = ((bf16[64,64,1024]{2,1,0:T(8,128)(2,1)}), bf16[64,64,1024]{2,1,0:T(8,128)(2,1)}, u32[]{:S(2)}, u32[]{:S(2)}) async-start(bf16[64,64,1024]{2,1,0:T(8,128)(2,1)} %stack.2), calls=%async_computation | async-start | bytes 16777216 | tf_op jit(solution)/shard_map/all_to_all | solution.py:11
  33.2 640.0 %all-gather.3.cloned.1.call-start = ((), (), s32[]{:S(2)}) async-start(), calls=%async_computation.2 | async-start | bytes 1064960 | tf_op jit(solution)/shard_map/all_gather | solution.py:24
  33.9 647.8 %all-gather.5.cloned.1.call-start = ((), (), s32[]{:S(2)}) async-start(), calls=%async_computation.3 | async-start | bytes 1064960 | tf_op jit(solution)/shard_map/all_gather | solution.py:25
  34.7 653.0 %reduce-scatter.2.cloned.1.call-start = ((), (), s32[]{:S(2)}) async-start(), calls=%async_computation.4 | async-start | bytes 4718592 | tf_op jit(solution)/shard_map/reduce_scatter | solution.py:55
  406.2 11.5 %copy-start.2 = (s32[64]{0:T(128)S(1)}, s32[64]{0:T(128)}, u32[]{:S(2)}) copy-start(s32[64]{0:T(128)} %param.10) | copy-start | bytes 772
  676.0 3.2 copy-start.1
Sparse Core Ops, SparseCore 0:
  37.3 156.0 all-gather.2
  196.7 161.1 all-gather.4
Sparse Core Ops, SparseCore 1:
  415.9 57.6 reduce-scatter.1
